TPU v7x, 256 devices: a whole 4x4x8 slice. The times are simulated.
256 devices in a mesh: row: 4 (over y), col: 64 (over z, x, core).
Axes of the slice: x: 4, y: 4, z: 8, core: 2. Of those that a mesh axis runs over, the one named last changes fastest.
Arguments:
- tokens: bfloat16 [32768, 4096], P(('row', 'col')), may hold values from -6 to 6
- expert_ids: int32 [32768, 2], P(('row', 'col')), may hold values from 0 to 63, all different within a row; in each aligned block of 128 rows (0 to 127, 128 to 255, ...) at most 5 rows name the same one
- gate_weights: float32 [32768, 2], P(('row', 'col')), may hold values from 0.1 to 1
- w_gate: bfloat16 [64, 4096, 1536], P('col', None, 'row'), may hold values from -0.09375 to 0.09375
- w_up: bfloat16 [64, 4096, 1536], P('col', None, 'row'), may hold values from -0.09375 to 0.09375
- w_down: bfloat16 [64, 1536, 4096], P('col', None, 'row'), may hold values from -0.15625 to 0.15625
Outputs:
- moe_out: bfloat16 [32768, 4096], P(('row', 'col'))
Inputs may be any that keep to these rules, and one draw needn't show every extreme that they name: `expert_ids`: each row names 2 different experts. Among the 128 rows of one device no expert is named by more than 5 rows, and in every draw some expert is named by exactly 5 rows of some device.
All inputs are finite; a program needn't handle non-finite values.
Results may differ from a plain program's by a relative error of at most 0.0058.
Values may be sent and summed in bfloat16 or wider, within the bound.
No kernel may reach another device: no remote copies, remote signals or barrier semaphores. Data moves between devices by JAX's collectives and lax.ppermute only.
A program may use at most 128 MiB of HBM per device.

v0:
```python
import jax
import jax.numpy as jnp
from jax import lax
from jax.sharding import PartitionSpec as P


def local(tokens, expert_ids, gate_weights, w_gate, w_up, w_down):
    token_count, top_count = expert_ids.shape
    width = tokens.shape[1]
    local_count = w_gate.shape[0]
    unit_count = w_gate.shape[2]
    quarter = w_down.shape[2]
    columns = lax.axis_size("col")
    groups = lax.axis_size("row")
    experts = local_count * columns
    capacity = max(2, token_count * top_count * 5 // (4 * experts))
    flat_ids = expert_ids.reshape(-1)
    onehot = (flat_ids[:, None] == jnp.arange(experts, dtype=jnp.int32)[None, :]).astype(jnp.int32)
    earlier = jnp.cumsum(onehot, axis=0) - onehot
    position = jnp.sum(earlier * onehot, axis=1)
    slot_ids = (flat_ids * capacity + position).reshape(token_count, top_count)
    chooser = jnp.any(
        jnp.arange(experts * capacity, dtype=jnp.int32)[:, None, None] == slot_ids[None, :, :],
        axis=2,
    ).astype(jnp.bfloat16)
    outgoing = jnp.dot(chooser, tokens, preferred_element_type=jnp.float32).astype(jnp.bfloat16)
    outgoing = outgoing.reshape(columns, local_count * capacity, width)
    arrived = lax.all_to_all(outgoing, "col", split_axis=0, concat_axis=0, tiled=True)
    block_rows = lax.all_gather(arrived[None], "row", axis=0, tiled=True)
    count = block_rows.shape[0]
    grouped = block_rows.reshape(count, columns, local_count, capacity, width)
    expert = 0
    inputs = grouped[:, :, expert].reshape(-1, width)
    gate_part = jnp.dot(inputs, w_gate[expert], preferred_element_type=jnp.float32)
    up_part = jnp.dot(inputs, w_up[expert], preferred_element_type=jnp.float32)
    hidden = (jax.nn.silu(gate_part) * up_part).astype(jnp.bfloat16)
    outputs = hidden.reshape(count, columns, 1, capacity, unit_count)
    hidden_all = outputs.reshape(count, columns, local_count * capacity, unit_count)
    hidden_split = hidden_all.reshape(groups, columns, local_count, capacity, unit_count)
    piece = lax.all_gather(hidden_split, "row", axis=4, tiled=True)
    count = piece.shape[4]
    expert = 0
    rows = piece[:, :, expert].reshape(-1, count)
    block = w_down[expert]
    parts = [jnp.dot(rows, block, preferred_element_type=jnp.float32)]
    summed = jnp.stack(parts)
    expert_out = summed.astype(jnp.bfloat16).reshape(
        local_count, groups, columns, capacity, quarter
    )
    expert_out = jnp.transpose(expert_out, (1, 2, 0, 3, 4)).reshape(
        groups, columns, local_count * capacity, quarter
    )
    colwise = lax.all_to_all(expert_out, "col", split_axis=1, concat_axis=1, tiled=True)
    home = lax.all_to_all(colwise, "row", split_axis=0, concat_axis=3, tiled=True)
    results = home.reshape(experts * capacity, width)
    shares = gate_weights / jnp.sum(gate_weights, axis=1, keepdims=True)
    picked = results[slot_ids].astype(jnp.float32)
    combined = jnp.sum(shares[:, :, None] * picked, axis=1)
    return combined.astype(jnp.bfloat16)


def solution(mesh):
    placed = (
        P(("row", "col"), None),
        P(("row", "col"), None),
        P(("row", "col"), None),
        P("col", None, "row"),
        P("col", None, "row"),
        P("col", None, "row"),
    )
    return jax.shard_map(
        local, mesh=mesh, in_specs=placed, out_specs=P(("row", "col"), None), check_vma=False
    )
```

profile of v0, /device:TPU:1, one launch (start us, length us, event | category | flops | bytes accessed | tf_op | source)
XLA Modules:
  0.0 528.3 jit_solution(9375818899468450079)
XLA Ops:
  6.5 0.9 copy.41
  7.6 0.1 eq.39
  7.8 0.6 reduce-window.6
  8.4 0.2 slice_reduce_fusion
  8.7 0.1 reduce_sum.31
  8.9 0.7 compare_select_fusion
  9.7 3.6 convolution_convert_fusion
  13.3 4.7 reshape.38
  18.0 107.6 %all_to_all.25 = bf16[64,5,4096]{2,1,0:T(8,128)(2,1)S(1)} all-to-all(bf16[64,5,4096]{2,1,0:T(8,128)(2,1)} %reshape.38), channel_id=1, replica_groups=mesh['row'=4,'col'=64] {'col'}, dimensions={0} | all-to-all | bytes 5242880 | tf_op jit(solution)/shard_map/all_to_all | solution.py:28
  125.6 3.2 copy.45
  128.8 0.3 all-gather.4.cloned.1.call-start
  129.2 101.0 %all-gather.6.cloned.1.call-done = bf16[256,5,4096]{2,0,1:T(8,128)(2,1)} async-done(((bf16[64,5,4096]{2,0,1:T(8,128)(2,1)}), bf16[256,5,4096]{2,0,1:T(8,128)(2,1)}) %all-gather.6.cloned.1.call-update) | async-done | bytes 10485776 | tf_op jit(solution)/shard_map/all_gather | solution.py:29
  230.2 15.2 %copy.46 = bf16[256,5,4096]{2,1,0:T(8,128)(2,1)} copy(bf16[256,5,4096]{2,0,1:T(8,128)(2,1)} %all-gather.6.cloned.1.call-done) | data formatting | bytes 20971520 | tf_op jit(solution)/shard_map/all_gather | solution.py:29
  245.4 16.8 %reshape_squeeze_reshape.3 = bf16[1280,4096]{1,0:T(8,128)(2,1)} reshape(bf16[256,5,4096]{2,1,0:T(8,128)(2,1)} %copy.46) | data formatting | bytes 20971520 | tf_op jit(solution)/shard_map/reshape;squeeze;reshape | solution.py:33
  262.3 9.3 %fusion.2 = f32[1280,384]{1,0:T(8,128)S(1)} fusion(bf16[1280,4096]{1,0:T(8,128)(2,1)} %reshape_squeeze_reshape.3, bf16[1,4096,384]{2,1,0:T(8,128)(2,1)} %param.9), kind=kOutput, calls=%fused_computation.7 | convolution fusion | flops 4026531840 | bytes 15597568 | tf_op jit(solution)/shard_map/dot_general | solution.py:34
  271.6 6.9 %fusion.4 = bf16[1280,384]{1,0:T(8,128)(2,1)} fusion(bf16[1280,4096]{1,0:T(8,128)(2,1)S(1)} %copy-done.1, bf16[1,4096,384]{2,1,0:T(8,128)(2,1)S(1)} %copy-done.3, f32[1280,384]{1,0:T(8,128)S(1)} %fusion.2), kind=kOutput, calls=%fused_computation.9 | convolution fusion | flops 4029480960 | bytes 16580608 | tf_op jit(solution)/shard_map/dot_general | solution.py:35
  278.6 3.0 reshape_reshape_reshape.3
  281.5 69.4 %all-gather.4.cloned.1.call-done = bf16[4,64,1,5,1536]{4,3,1,0,2:T(8,128)(2,1)} async-done(((bf16[4,64,1,5,384]{4,3,1,0,2:T(8,128)(2,1)}), bf16[4,64,1,5,1536]{4,3,1,0,2:T(8,128)(2,1)}) %all-gather.4.cloned.1.call-update) | async-done | bytes 3932176 | tf_op jit(solution)/shard_map/all_gather | solution.py:40
  351.0 7.6 %reshape_squeeze.3 = bf16[1280,1536]{1,0:T(8,128)(2,1)} reshape(bf16[4,64,1,5,1536]{4,3,1,0,2:T(8,128)(2,1)} %all-gather.4.cloned.1.call-done) | data formatting | bytes 7864320 | tf_op jit(solution)/shard_map/reshape;squeeze | solution.py:43
  358.6 7.6 %convolution_convert_fusion.1 = bf16[1280,1024]{1,0:T(8,128)(2,1)} fusion(bf16[1280,1536]{1,0:T(8,128)(2,1)} %reshape_squeeze.3, bf16[1,1536,1024]{2,1,0:T(8,128)(2,1)S(1)} %copy-done), kind=kOutput, calls=%fused_computation.3 | convolution fusion | flops 4027842560 | bytes 9699328 | tf_op jit(solution)/shard_map/dot_general | solution.py:45
  366.2 6.5 %reshape_transpose_reshape.3 = bf16[4,64,5,1024]{3,2,1,0:T(8,128)(2,1)} reshape(bf16[1280,1024]{1,0:T(8,128)(2,1)} %convolution_convert_fusion.1) | data formatting | bytes 5242880 | tf_op jit(solution)/shard_map/reshape;transpose;reshape | solution.py:50
  372.8 7.3 %copy.47 = bf16[4,64,5,1024]{3,0,2,1:T(4,128)(2,1)S(1)} copy(bf16[4,64,5,1024]{3,2,1,0:T(8,128)(2,1)} %reshape_transpose_reshape.3) | data formatting | bytes 5242880 | tf_op jit(solution)/shard_map/reshape;transpose;reshape | solution.py:50
  380.1 73.2 %all_to_all.26 = bf16[4,64,5,1024]{3,0,2,1:T(4,128)(2,1)S(1)} all-to-all(bf16[4,64,5,1024]{3,0,2,1:T(4,128)(2,1)S(1)} %copy.47), channel_id=1, replica_groups=mesh['row'=4,'col'=64] {'col'}, dimensions={1} | all-to-all | bytes 5242880 | tf_op jit(solution)/shard_map/all_to_all | solution.py:53
  453.3 2.3 copy.48
  455.7 4.8 all-to-all-start.2
  460.6 0.1 reshape.42
  460.9 31.4 %all-to-all-done.2 = bf16[4,64,5,1024]{3,1,2,0:T(8,128)(2,1)} async-done(((bf16[4,64,5,1024]{3,1,2,0:T(8,128)(2,1)}), bf16[4,64,5,1024]{3,1,2,0:T(8,128)(2,1)}, u32[]{:S(2)}, u32[]{:S(2)}) %all-to-all-start.2) | async-done | bytes 2621472 | tf_op jit(solution)/shard_map/all_to_all | solution.py:54
  492.3 3.8 copy.49
  496.0 2.6 copy.52
  498.7 7.3 %gather_fusion = bf16[256,4096]{1,0:T(8,128)(2,1)} fusion(bf16[320,4096]{1,0:T(8,128)(2,1)} %bitcast.43, s32[1024]{0:T(1024)S(1)} %pad_clamp_fusion), kind=kCustom, calls=%fused_computation | custom fusion | bytes 4195328 | tf_op jit(solution)/shard_map/gather | solution.py:57
  506.0 5.6 %reshape.52 = f32[128,2,4096]{2,1,0:T(2,128)} reshape(bf16[256,4096]{1,0:T(8,128)(2,1)} %gather_fusion) | data formatting | bytes 6291456 | tf_op jit(solution)/shard_map/convert_element_type | solution.py:57
  511.6 9.6 %multiply_reduce_fusion = bf16[128,4096]{1,0:T(8,128)(2,1)} fusion(f32[128,2,4096]{2,1,0:T(2,128)} %reshape.52, f32[128,2]{1,0:T(8,128)S(1)} %copy.40), kind=kLoop, calls=%fused_computation.2 | loop fusion | flops 1572864 | bytes 5243904 | tf_op jit(solution)/shard_map/reduce_sum | solution.py:58
  (23 shorter events, 0.7 us)
Async XLA Ops:
  6.5 352.1 %copy-start = (bf16[1,1536,1024]{2,1,0:T(8,128)(2,1)S(1)}, bf16[1,1536,1024]{2,1,0:T(8,128)(2,1)}, u32[]{:S(2)}) copy-start(bf16[1,1536,1024]{2,1,0:T(8,128)(2,1)} %param.11) | copy-start | bytes 9437188
  6.5 223.7 %all-gather.6.cloned.1.call-start = ((), (), s32[]{:S(2)}) async-start(), calls=%async_computation.4 | async-start | bytes 13107200 | tf_op jit(solution)/shard_map/all_gather | solution.py:29
  128.8 222.1 %all-gather.4.cloned.1.call-start = ((), (), s32[]{:S(2)}) async-start(), calls=%async_computation.3 | async-start | bytes 7864320 | tf_op jit(solution)/shard_map/all_gather | solution.py:40
  262.3 9.4 %copy-start.1 = (bf16[1280,4096]{1,0:T(8,128)(2,1)S(1)}, bf16[1280,4096]{1,0:T(8,128)(2,1)}, u32[]{:S(2)}) copy-start(bf16[1280,4096]{1,0:T(8,128)(2,1)} %reshape_squeeze_reshape.3) | copy-start | bytes 31457284
  262.3 9.4 %copy-start.3 = (bf16[1,4096,384]{2,1,0:T(8,128)(2,1)S(1)}, bf16[1,4096,384]{2,1,0:T(8,128)(2,1)}, u32[]{:S(2)}) copy-start(bf16[1,4096,384]{2,1,0:T(8,128)(2,1)} %param.10) | copy-start | bytes 9437188
  455.6 5.1 copy-start.2
  455.7 36.6 %all-to-all-start.2 = ((bf16[4,64,5,1024]{3,1,2,0:T(8,128)(2,1)}), bf16[4,64,5,1024]{3,1,2,0:T(8,128)(2,1)}, u32[]{:S(2)}, u32[]{:S(2)}) async-start(bf16[4,64,5,1024]{3,1,2,0:T(8,128)(2,1)} %copy.48), calls=%async_computation.2 | async-start | bytes 5242880 | tf_op jit(solution)/shard_map/all_to_all | solution.py:54
Sparse Core Ops, SparseCore 0:
  128.9 101.2 all-gather.5
  281.7 69.2 all-gather.3
where the time goes:
time: 534 us; the launch traced here: 528 us
  waiting for transfers between devices  202 us (38%)
  blocking collectives  181 us (34%)
  local copies, waits for them, and re-layouts  88.1 us (16%)
  matrix products  27.4 us (5%)
  between operations  13.7 us (3%)
  other arithmetic  11.2 us (2%)
    all_to_all x1, blocking collectives, local(): lax.all_to_all(outgoing, 'col', split_axis=0, concat_axis=0, tiled=True)  108 us
    all_gather x1, waiting for transfers between devices, local(): block_rows = lax.all_gather(arrived[None], 'row', axis=0, tiled=True)  101 us
    all_to_all x1, blocking collectives, local(): lax.all_to_all(expert_out, 'col', split_axis=1, concat_axis=1, tiled=True)  73.2 us
    all_gather x1, waiting for transfers between devices, local(): piece = lax.all_gather(hidden_split, 'row', axis=4, tiled=True)  69.4 us
    all_to_all x1, waiting for transfers between devices, local(): lax.all_to_all(colwise, 'row', split_axis=0, concat_axis=3, tiled=True)  31.4 us
    another operation x1, local copies, waits for them, and re-layouts, local(): inputs = grouped[:, :, expert].reshape(-1, width)  16.8 us
    all_gather x1, local copies, waits for them, and re-layouts, local(): block_rows = lax.all_gather(arrived[None], 'row', axis=0, tiled=True)  15.2 us
    another operation x2, local copies, waits for them, and re-layouts, local(): jnp.transpose(expert_out, (1, 2, 0, 3, 4))  13.9 us
  transfers between devices with their start and end apart: 3, of which 3 were waited for; matrix products, arithmetic and copies ran while one was open for 0% of the time, Pallas kernels for 0%

commit v1 on v0

--- a/solution.py
+++ b/solution.py
@@ -50,7 +50,10 @@
     expert_out = jnp.transpose(expert_out, (1, 2, 0, 3, 4)).reshape(
         groups, columns, local_count * capacity, quarter
     )
-    colwise = lax.all_to_all(expert_out, "col", split_axis=1, concat_axis=1, tiled=True)
+    colwise = jnp.concatenate(
+        lax.all_to_all(jnp.stack(jnp.split(expert_out, lax.axis_size("col"), axis=1)), "col", 0, 0),
+        axis=1,
+    )
     home = lax.all_to_all(colwise, "row", split_axis=0, concat_axis=3, tiled=True)
     results = home.reshape(experts * capacity, width)
     shares = gate_weights / jnp.sum(gate_weights, axis=1, keepdims=True)

time: 534 us -> 588 us (1.10)
  local copies, waits for them, and re-layouts: 88.1 us -> 140 us
    unnamed x10 -> x73, local copies, waits for them, and re-layouts: 3.59 us -> 56.7 us
    another operation x2 -> x1, local copies, waits for them, and re-layouts: 13.9 us -> 6.54 us  [local(): jnp.transpose(expert_out, (1, 2, 0, 3, 4))]
    another operation x1 -> x3, local copies, waits for them, and re-layouts: 0.01 us -> 6 us  [the longest x2 6 us: local(): jnp.stack(jnp.split(expert_out, lax.axis_size('col'), axis=1))]
where the time goes in v1:
time: 588 us; the launch traced here: 580 us
  waiting for transfers between devices  202 us (34%)
  blocking collectives  181 us (31%)
  local copies, waits for them, and re-layouts  140 us (24%)
  matrix products  27.4 us (5%)
  between operations  13.8 us (2%)
  other arithmetic  11.2 us (2%)
    all_to_all x1, blocking collectives, local(): lax.all_to_all(outgoing, 'col', split_axis=0, concat_axis=0, tiled=True)  108 us
    all_gather x1, waiting for transfers between devices, local(): block_rows = lax.all_gather(arrived[None], 'row', axis=0, tiled=True)  101 us
    all_to_all x1, blocking collectives, local(): lax.all_to_all(jnp.stack(jnp.split(expert_out, lax.axis_size('col'), axis...  73.2 us
    all_gather x1, waiting for transfers between devices, local(): piece = lax.all_gather(hidden_split, 'row', axis=4, tiled=True)  69.4 us
    unnamed x73, local copies, waits for them, and re-layouts  56.7 us
    all_to_all x1, waiting for transfers between devices, local(): lax.all_to_all(colwise, 'row', split_axis=0, concat_axis=3, tiled=True)  31.4 us
    another operation x1, local copies, waits for them, and re-layouts, local(): inputs = grouped[:, :, expert].reshape(-1, width)  16.8 us
    all_gather x1, local copies, waits for them, and re-layouts, local(): block_rows = lax.all_gather(arrived[None], 'row', axis=0, tiled=True)  15.2 us
  transfers between devices with their start and end apart: 3, of which 3 were waited for; matrix products, arithmetic and copies ran while one was open for 0% of the time, Pallas kernels for 0%

profile of v1, /device:TPU:1, one launch (start us, length us, event | category | flops | bytes accessed | tf_op | source)
XLA Modules:
  0.0 580.0 jit_solution(10471791807503010292)
XLA Ops:
  6.5 0.9 copy.293
  9.7 3.6 convolution_convert_fusion
  13.3 4.7 reshape.44
  18.0 107.6 %all_to_all.25 = bf16[64,5,4096]{2,1,0:T(8,128)(2,1)S(1)} all-to-all(bf16[64,5,4096]{2,1,0:T(8,128)(2,1)} %reshape.44), channel_id=1, replica_groups=mesh['row'=4,'col'=64] {'col'}, dimensions={0} | all-to-all | bytes 5242880 | tf_op jit(solution)/shard_map/all_to_all | solution.py:28
  125.6 3.2 copy.297
  129.2 101.0 %all-gather.6.cloned.1.call-done = bf16[256,5,4096]{2,0,1:T(8,128)(2,1)} async-done(((bf16[64,5,4096]{2,0,1:T(8,128)(2,1)}), bf16[256,5,4096]{2,0,1:T(8,128)(2,1)}) %all-gather.6.cloned.1.call-update) | async-done | bytes 10485776 | tf_op jit(solution)/shard_map/all_gather | solution.py:29
  230.2 15.2 %copy.298 = bf16[256,5,4096]{2,1,0:T(8,128)(2,1)} copy(bf16[256,5,4096]{2,0,1:T(8,128)(2,1)} %all-gather.6.cloned.1.call-done) | data formatting | bytes 20971520 | tf_op jit(solution)/shard_map/all_gather | solution.py:29
  245.4 16.8 %reshape_squeeze_reshape.3 = bf16[1280,4096]{1,0:T(8,128)(2,1)} reshape(bf16[256,5,4096]{2,1,0:T(8,128)(2,1)} %copy.298) | data formatting | bytes 20971520 | tf_op jit(solution)/shard_map/reshape;squeeze;reshape | solution.py:33
  262.3 9.3 %fusion.2 = f32[1280,384]{1,0:T(8,128)S(1)} fusion(bf16[1280,4096]{1,0:T(8,128)(2,1)} %reshape_squeeze_reshape.3, bf16[1,4096,384]{2,1,0:T(8,128)(2,1)} %param.9), kind=kOutput, calls=%fused_computation.7 | convolution fusion | flops 4026531840 | bytes 15597568 | tf_op jit(solution)/shard_map/dot_general | solution.py:34
  271.6 6.9 %fusion.4 = bf16[1280,384]{1,0:T(8,128)(2,1)} fusion(bf16[1280,4096]{1,0:T(8,128)(2,1)S(1)} %copy-done.1, bf16[1,4096,384]{2,1,0:T(8,128)(2,1)S(1)} %copy-done.3, f32[1280,384]{1,0:T(8,128)S(1)} %fusion.2), kind=kOutput, calls=%fused_computation.9 | convolution fusion | flops 4029480960 | bytes 16580608 | tf_op jit(solution)/shard_map/dot_general | solution.py:35
  278.6 3.0 reshape_reshape_reshape.3
  281.5 69.4 %all-gather.4.cloned.1.call-done = bf16[4,64,1,5,1536]{4,3,1,0,2:T(8,128)(2,1)} async-done(((bf16[4,64,1,5,384]{4,3,1,0,2:T(8,128)(2,1)}), bf16[4,64,1,5,1536]{4,3,1,0,2:T(8,128)(2,1)}) %all-gather.4.cloned.1.call-update) | async-done | bytes 3932176 | tf_op jit(solution)/shard_map/all_gather | solution.py:40
  351.0 7.6 %reshape_squeeze.3 = bf16[1280,1536]{1,0:T(8,128)(2,1)} reshape(bf16[4,64,1,5,1536]{4,3,1,0,2:T(8,128)(2,1)} %all-gather.4.cloned.1.call-done) | data formatting | bytes 7864320 | tf_op jit(solution)/shard_map/reshape;squeeze | solution.py:43
  358.6 7.6 %convolution_convert_fusion.1 = bf16[1280,1024]{1,0:T(8,128)(2,1)} fusion(bf16[1280,1536]{1,0:T(8,128)(2,1)} %reshape_squeeze.3, bf16[1,1536,1024]{2,1,0:T(8,128)(2,1)S(1)} %copy-done), kind=kOutput, calls=%fused_computation.3 | convolution fusion | flops 4027842560 | bytes 9699328 | tf_op jit(solution)/shard_map/dot_general | solution.py:45
  366.2 6.5 %reshape_transpose_reshape.3 = bf16[4,64,5,1024]{3,2,1,0:T(8,128)(2,1)} reshape(bf16[1280,1024]{1,0:T(8,128)(2,1)} %convolution_convert_fusion.1) | data formatting | bytes 5242880 | tf_op jit(solution)/shard_map/reshape;transpose;reshape | solution.py:50
  372.8 0.8 constant_dynamic-update-slice_fusion.63
  374.5 0.8 constant_dynamic-update-slice_fusion.61
  385.4 0.8 constant_dynamic-update-slice_fusion.48
  387.1 0.8 constant_dynamic-update-slice_fusion.46
  388.8 0.8 constant_dynamic-update-slice_fusion.44
  390.5 0.8 constant_dynamic-update-slice_fusion.42
  401.5 0.8 constant_dynamic-update-slice_fusion.29
  426.8 5.2 copy.362
  431.9 73.2 %all_to_all.26 = bf16[64,4,1,5,1024]{4,1,3,2,0:T(4,128)(2,1)S(1)} all-to-all(bf16[64,4,1,5,1024]{4,1,3,2,0:T(4,128)(2,1)S(1)} %copy.362), channel_id=1, replica_groups=mesh['row'=4,'col'=64] {'col'}, dimensions={0} | all-to-all | bytes 5242880 | tf_op jit(solution)/shard_map/all_to_all | solution.py:54
  505.2 2.3 copy.363
  507.5 4.7 all-to-all-start.2
  512.6 31.4 %all-to-all-done.2 = bf16[4,64,5,1024]{3,1,2,0:T(8,128)(2,1)} async-done(((bf16[4,64,5,1024]{3,1,2,0:T(8,128)(2,1)}), bf16[4,64,5,1024]{3,1,2,0:T(8,128)(2,1)}, u32[]{:S(2)}, u32[]{:S(2)}) %all-to-all-start.2) | async-done | bytes 2621472 | tf_op jit(solution)/shard_map/all_to_all | solution.py:57
  544.0 3.8 copy.364
  547.8 2.6 copy.430
  550.4 7.3 %gather_fusion = bf16[256,4096]{1,0:T(8,128)(2,1)} fusion(bf16[320,4096]{1,0:T(8,128)(2,1)} %bitcast.428, s32[1024]{0:T(1024)S(1)} %pad_clamp_fusion), kind=kCustom, calls=%fused_computation | custom fusion | bytes 4195328 | tf_op jit(solution)/shard_map/gather | solution.py:60
  557.7 5.6 reshape.60
  563.3 9.6 %multiply_reduce_fusion = bf16[128,4096]{1,0:T(8,128)(2,1)} fusion(f32[128,2,4096]{2,1,0:T(2,128)} %reshape.60, f32[128,2]{1,0:T(8,128)S(1)} %copy.292), kind=kLoop, calls=%fused_computation.2 | loop fusion | flops 1572864 | bytes 5243904 | tf_op jit(solution)/shard_map/reduce_sum | solution.py:61
  (87 shorter events, 51.0 us)
Async XLA Ops:
  6.5 352.1 %copy-start = (bf16[1,1536,1024]{2,1,0:T(8,128)(2,1)S(1)}, bf16[1,1536,1024]{2,1,0:T(8,128)(2,1)}, u32[]{:S(2)}) copy-start(bf16[1,1536,1024]{2,1,0:T(8,128)(2,1)} %param.11) | copy-start | bytes 9437188
  6.5 223.7 %all-gather.6.cloned.1.call-start = ((), (), s32[]{:S(2)}) async-start(), calls=%async_computation.4 | async-start | bytes 13107200 | tf_op jit(solution)/shard_map/all_gather | solution.py:29
  128.8 222.1 %all-gather.4.cloned.1.call-start = ((), (), s32[]{:S(2)}) async-start(), calls=%async_computation.3 | async-start | bytes 7864320 | tf_op jit(solution)/shard_map/all_gather | solution.py:40
  262.3 9.4 %copy-start.1 = (bf16[1280,4096]{1,0:T(8,128)(2,1)S(1)}, bf16[1280,4096]{1,0:T(8,128)(2,1)}, u32[]{:S(2)}) copy-start(bf16[1280,4096]{1,0:T(8,128)(2,1)} %reshape_squeeze_reshape.3) | copy-start | bytes 31457284
  262.3 9.4 %copy-start.3 = (bf16[1,4096,384]{2,1,0:T(8,128)(2,1)S(1)}, bf16[1,4096,384]{2,1,0:T(8,128)(2,1)}, u32[]{:S(2)}) copy-start(bf16[1,4096,384]{2,1,0:T(8,128)(2,1)} %param.10) | copy-start | bytes 9437188
  505.1 7.3 %copy-start.2 = (f32[128,2]{0,1:T(2,128)S(1)}, f32[128,2]{0,1:T(2,128)}, u32[]{:S(2)}) copy-start(f32[128,2]{0,1:T(2,128)} %param.8) | copy-start | bytes 3076
  507.5 36.5 %all-to-all-start.2 = ((bf16[4,64,5,1024]{3,1,2,0:T(8,128)(2,1)}), bf16[4,64,5,1024]{3,1,2,0:T(8,128)(2,1)}, u32[]{:S(2)}, u32[]{:S(2)}) async-start(bf16[4,64,5,1024]{3,1,2,0:T(8,128)(2,1)} %copy.363), calls=%async_computation.2 | async-start | bytes 5242880 | tf_op jit(solution)/shard_map/all_to_all | solution.py:57
Sparse Core Ops, SparseCore 0:
  128.9 101.2 all-gather.5
  281.7 69.2 all-gather.3
